TPU v7x, 128 devices: a whole 4x4x4 slice. The times are simulated.
128 devices in a mesh: req: 16 (over z, x), head: 8 (over y, core).
Axes of the slice: x: 4, y: 4, z: 4, core: 2. Of those that a mesh axis runs over, the one named last changes fastest.
Arguments:
- tokens: bfloat16 [256, 1280], P('req'), may hold values from -6 to 6
- w_qkv: bfloat16 [2, 3, 1280, 1280], P(None, None, 'head'), may hold values from -0.15625 to 0.15625
- w_out: bfloat16 [2, 1280, 1280], P(None, 'head'), may hold values from -0.15625 to 0.15625
- w_up: bfloat16 [2, 1280, 1280], P(None, 'head'), may hold values from -0.15625 to 0.15625
- w_down: bfloat16 [2, 1280, 1280], P(None, 'head'), may hold values from -0.15625 to 0.15625
- gain_attn: float32 [2, 1280], replicated, may hold values from 0.1 to 1.9
- gain_mlp: float32 [2, 1280], replicated, may hold values from 0.1 to 1.9
- suffix_cache: bfloat16 [2, 2, 512, 1280, 128], P(None, None, 'req', 'head'), may hold values from -110 to 110
- prompt_cache: bfloat16 [2, 2, 96, 1280, 128], P(None, None, 'req', 'head'), may hold values from -110 to 110
- suffix_table: int32 [16, 32], P('req'), may hold values from 0 to 31, each once within a row
- prompt_owner: int32 [96], replicated, may hold values from 0 to 95, each once
- suffix_len: int32 [256], P('req'), may hold values from 1 to 256, 32768 in all
- group_id: int32 [256], P('req'), may hold values from 0 to 23, never falling along the last dimension, each value on 1 to 16 neighbouring positions
Outputs:
- hidden: bfloat16 [256, 1280], P('req')
- new_cache: bfloat16 [2, 2, 256, 1280], P(None, None, 'req', 'head')
Inputs may be any that keep to these rules, and one draw needn't show every extreme that they name: `suffix_table`: each row holds every number once. `prompt_owner`: each number once. `group_id`: never falls from one request to the next; every group has 1 to 16 requests, one group exactly 16.
All inputs are finite; a program needn't handle non-finite values. No bound on the sum of `suffix_len` on one device may be relied on, other than what follows from the above.
Results may differ from a plain program's by a relative error of at most 0.019.
The roundings to bfloat16 on the way count: a program that leaves them out, or rounds other values in their place, can miss the bound.
Values may be sent and summed in bfloat16 or wider, within the bound.
No kernel may reach another device: no remote copies, remote signals or barrier semaphores. Data moves between devices by JAX's collectives and lax.ppermute only.
A program may use at most 128 MiB of HBM per device.

v0:
```python
import math
import jax
import jax.numpy as jnp
from jax import lax
from jax.sharding import PartitionSpec as P

HD = 80
PPAGES = 4
NEG_FLOOR = -1e30


def root_norm(values, gains):
    factor = lax.rsqrt(jnp.mean(values * values, axis=-1, keepdims=True) + 1e-06)
    return values * factor * gains


def page_groups(prompt_owner, count, page_len):
    owners = prompt_owner // PPAGES
    return jnp.repeat(owners, page_len, total_repeat_length=count * page_len)


def attend(
    query, key_new, val_new, layer_suffix, layer_prompt, pages, valid, group_id, prompt_owner
):
    row_count = query.shape[0]
    head_count = query.shape[1] // HD
    scale = 1.0 / math.sqrt(HD)
    page_len = layer_suffix.shape[3]
    own_pages = pages.shape[1]
    query_heads = query.reshape(row_count, head_count, HD)
    key_heads = key_new.reshape(row_count, head_count, HD)
    val_heads = val_new.reshape(row_count, head_count, HD)
    gathered_pages = layer_suffix[:, pages].reshape(
        2, row_count, own_pages, head_count, HD, page_len
    )
    scores = (
        jnp.einsum(
            "rhd,rphdt->rhpt", query_heads, gathered_pages[0], preferred_element_type=jnp.float32
        ).reshape(row_count, head_count, own_pages * page_len)
        * scale
    )
    own = (
        jnp.einsum("rhd,rhd->rh", query_heads, key_heads, preferred_element_type=jnp.float32)
        * scale
    )
    mask = valid[:, None, :]
    local_top = jnp.maximum(jnp.max(jnp.where(mask, scores, NEG_FLOOR), axis=-1), own)
    weights = jnp.exp(jnp.where(mask, scores - local_top[..., None], NEG_FLOOR))
    own_weight = jnp.exp(own - local_top)
    total = jnp.sum(weights, axis=-1) + own_weight
    weight_pages = weights.astype(jnp.bfloat16).reshape(row_count, head_count, own_pages, page_len)
    mixed = jnp.einsum(
        "rhpt,rphdt->rhd", weight_pages, gathered_pages[1], preferred_element_type=jnp.float32
    )
    mixed = mixed + jnp.einsum(
        "rh,rhd->rhd",
        own_weight.astype(jnp.bfloat16),
        val_heads,
        preferred_element_type=jnp.float32,
    )
    piece = lax.all_gather(layer_prompt, "req", axis=1, tiled=True)
    count = piece.shape[1]
    key_group = page_groups(prompt_owner, count, page_len)
    keys = piece[0].reshape(count, head_count, HD, page_len)
    vals = piece[1].reshape(count, head_count, HD, page_len)
    block = (
        jnp.einsum("rhd,phdt->rhpt", query_heads, keys, preferred_element_type=jnp.float32).reshape(
            row_count, head_count, count * page_len
        )
        * scale
    )
    match = (group_id[:, None] == key_group[None, :])[:, None, :]
    new_top = jnp.maximum(local_top, jnp.max(jnp.where(match, block, NEG_FLOOR), axis=-1))
    block_weights = jnp.exp(jnp.where(match, block - new_top[..., None], NEG_FLOOR))
    factor = jnp.exp(local_top - new_top)
    new_total = total * factor + jnp.sum(block_weights, axis=-1)
    block_rounded = block_weights.astype(jnp.bfloat16).reshape(
        row_count, head_count, count, page_len
    )
    new_mixed = mixed * factor[..., None] + jnp.einsum(
        "rhpt,phdt->rhd", block_rounded, vals, preferred_element_type=jnp.float32
    )
    return (new_mixed / new_total[..., None]).reshape(row_count, -1).astype(jnp.bfloat16)


def add_branch(residual, partial_value, gains, closing):
    residual = residual + lax.psum(partial_value, "head")
    if closing:
        normed = None
    else:
        normed = root_norm(residual, gains).astype(jnp.bfloat16)
    return (residual, normed)


def local(
    tokens,
    w_qkv,
    w_out,
    w_up,
    w_down,
    gain_attn,
    gain_mlp,
    suffix_cache,
    prompt_cache,
    suffix_table,
    prompt_owner,
    suffix_len,
    group_id,
):
    row_count = tokens.shape[0]
    layer_count = w_qkv.shape[0]
    width_here = w_qkv.shape[2]
    model_width = w_qkv.shape[3]
    pages = suffix_table[0].reshape(row_count, -1)
    span = pages.shape[1] * suffix_cache.shape[4]
    valid = jnp.arange(span, dtype=jnp.int32)[None, :] < suffix_len[:, None]
    whole = tokens.astype(jnp.float32)
    normed = root_norm(whole, gain_attn[0]).astype(jnp.bfloat16)
    residual = whole
    new_keys = []
    new_vals = []
    for layer in range(layer_count):
        projected = jnp.einsum(
            "rd,kd->rk",
            normed,
            w_qkv[layer].reshape(3 * width_here, model_width),
            preferred_element_type=jnp.float32,
        )
        projected = projected.reshape(row_count, 3, width_here).astype(jnp.bfloat16)
        query = projected[:, 0]
        key_new = projected[:, 1]
        val_new = projected[:, 2]
        new_keys.append(key_new)
        new_vals.append(val_new)
        attended = attend(
            query,
            key_new,
            val_new,
            suffix_cache[layer],
            prompt_cache[layer],
            pages,
            valid,
            group_id,
            prompt_owner,
        )
        partial_value = jnp.dot(attended, w_out[layer], preferred_element_type=jnp.float32)
        residual, normed = add_branch(residual, partial_value, gain_mlp[layer], False)
        hidden_units = jax.nn.silu(
            jnp.einsum("rd,fd->rf", normed, w_up[layer], preferred_element_type=jnp.float32)
        ).astype(jnp.bfloat16)
        partial_value = jnp.dot(hidden_units, w_down[layer], preferred_element_type=jnp.float32)
        closing = layer == layer_count - 1
        next_gains = gain_attn[layer] if closing else gain_attn[layer + 1]
        residual, normed = add_branch(residual, partial_value, next_gains, closing)
    hidden = residual.astype(jnp.bfloat16)
    new_cache = jnp.stack([jnp.stack(new_keys), jnp.stack(new_vals)], axis=1)
    return (hidden, new_cache)


def solution(mesh):
    placed = (
        P("req", None),
        P(None, None, "head", None),
        P(None, "head", None),
        P(None, "head", None),
        P(None, "head", None),
        P(),
        P(),
        P(None, None, "req", "head", None),
        P(None, None, "req", "head", None),
        P("req", None),
        P(),
        P("req"),
        P("req"),
    )
    return jax.shard_map(
        local,
        mesh=mesh,
        in_specs=placed,
        out_specs=(P("req", None), P(None, None, "req", "head")),
        check_vma=False,
    )
```

profile of v0, /device:TPU:1, one launch (start us, length us, event | category | flops | bytes accessed | tf_op | source)
XLA Modules:
  0.0 431.9 jit_solution(11187171101283764259)
XLA Ops:
  7.3 2.4 fusion.147
  9.8 0.1 fusion.94
  9.9 0.5 fusion.38
  10.4 0.1 reshape_squeeze.31
  10.7 0.1 fusion.125
  10.8 0.5 broadcast.282
  11.4 0.7 reduce.26
  12.3 73.0 %gather_fusion.2 = s32[12288]{0:T(1024)S(1)} fusion(s32[96]{0:T(128)S(1)} %and_select_fusion, s32[12288]{0:T(1024)S(1)} %fusion.97), kind=kCustom, calls=%fused_computation.clone | custom fusion | bytes 147456 | tf_op jit(solution)/shard_map/jit(_take)/gather | solution.py:19
  85.4 4.6 %slice_bitcast_fusion = (bf16[2,32,160,128]{3,2,1,0:T(8,128)(2,1)S(1)}, bf16[2,32,160,128]{3,2,1,0:T(8,128)(2,1)}) fusion(bf16[2,2,32,160,128]{4,3,2,1,0:T(8,128)(2,1)} %param.26), kind=kLoop, calls=%fused_computation.11 | loop fusion | bytes 10485760 | tf_op jit(solution)/shard_map/squeeze | solution.py:139
  90.0 4.1 gather_fusion
  94.2 1.9 fusion.146
  96.1 0.3 fusion.26
  96.4 0.1 select_reduce_fusion.1
  96.5 0.2 fusion.116
  96.7 0.2 broadcast_compare_fusion
  96.9 0.4 fusion.24
  97.3 3.6 fusion.144
  101.0 0.8 fusion.11
  101.7 0.5 fusion.28
  102.3 1.2 fusion.62
  103.6 1.8 fusion.86
  105.5 0.7 all-gather.7.cloned.1.call-update
  106.3 2.4 gather_fusion.1
  108.8 3.0 fusion.145
  111.8 53.2 %all-reduce.5.cloned.1.call-done = f32[16,1280]{1,0:T(8,128)} async-done(((f32[16,1280]{1,0:T(8,128)}), f32[16,1280]{1,0:T(8,128)}) %all-reduce.5.cloned.1.call-update) | async-done | bytes 81936 | tf_op jit(solution)/shard_map/psum | solution.py:87
  165.0 1.0 multiply_reduce_fusion.2
  166.1 2.2 fusion.82
  168.3 67.2 %all-gather.7.cloned.1.call-done = bf16[1,2,96,160,128]{4,3,2,1,0:T(8,128)(2,1)} async-done(((bf16[1,2,6,160,128]{4,3,2,1,0:T(8,128)(2,1)}), bf16[1,2,96,160,128]{4,3,2,1,0:T(8,128)(2,1)}) %all-gather.7.cloned.1.call-update) | async-done | bytes 7864336 | tf_op jit(solution)/shard_map/all_gather | solution.py:61
  235.5 5.4 %fusion.143 = (bf16[1,1,96,160,128]{4,3,2,1,0:T(8,128)(2,1)}, bf16[1,1,96,160,128]{4,3,2,1,0:T(8,128)(2,1)}) fusion(bf16[1,2,96,160,128]{4,3,2,1,0:T(8,128)(2,1)} %all-gather.7.cloned.1.call-done), kind=kLoop, calls=%fused_computation.177 | loop fusion | bytes 15728640 | tf_op jit(solution)/shard_map/slice | solution.py:64
  241.0 52.7 %all-reduce.7.cloned.1.call-done = f32[16,1280]{1,0:T(8,128)} async-done(((f32[16,1280]{1,0:T(8,128)}), f32[16,1280]{1,0:T(8,128)}) %all-reduce.7.cloned.1.call-update) | async-done | bytes 81936 | tf_op jit(solution)/shard_map/psum | solution.py:87
  293.7 1.0 multiply_reduce_fusion.1
  294.7 1.7 fusion.41
  296.4 0.1 reshape_squeeze.36
  296.7 0.1 fusion.123
  296.9 0.3 fusion.22
  297.2 0.1 select_reduce_fusion
  297.3 0.2 fusion.118
  297.5 2.9 fusion.8
  300.4 1.7 fusion.20
  302.2 0.6 fusion.30
  302.7 3.3 fusion.65
  306.2 1.8 fusion.80
  308.1 56.1 %all-reduce.9.cloned.1.call-done = f32[16,1280]{1,0:T(8,128)} async-done(((f32[16,1280]{1,0:T(8,128)}), f32[16,1280]{1,0:T(8,128)}) %all-reduce.9.cloned.1.call-update) | async-done | bytes 81936 | tf_op jit(solution)/shard_map/psum | solution.py:87
  364.2 1.0 multiply_reduce_fusion
  365.2 2.2 fusion.76
  367.4 0.6 copy.45
  368.0 55.5 %all-reduce.11.cloned.1.call-done = f32[16,1280]{1,0:T(8,128)} async-done(((f32[16,1280]{1,0:T(8,128)}), f32[16,1280]{1,0:T(8,128)}) %all-reduce.11.cloned.1.call-update) | async-done | bytes 81936 | tf_op jit(solution)/shard_map/psum | solution.py:87
  423.5 1.5 add_convert_fusion
  (69 shorter events, 1.7 us)
Async XLA Ops:
  7.2 2.6 copy-start.4
  7.2 2.6 copy-start.2
  7.2 2.7 copy-start.3
  7.2 4.2 copy-start.8
  7.2 90.1 %all-gather.5.cloned.1.call-start = ((), (), s32[]{:S(2)}) async-start(), calls=%async_computation.4 | async-start | bytes 8355840 | tf_op jit(solution)/shard_map/all_gather | solution.py:61
  9.6 2.7 copy-start.9
  9.7 155.4 %all-reduce.5.cloned.1.call-start = ((), (), s32[]{:S(2)}) async-start(), calls=%async_computation | async-start | bytes 163840 | tf_op jit(solution)/shard_map/psum | solution.py:87
  90.0 4.2 copy-start.7
  94.2 2.5 copy-start.6
  105.5 130.1 %all-gather.7.cloned.1.call-start = ((), (), s32[]{:S(2)}) async-start(), calls=%async_computation.5 | async-start | bytes 8355840 | tf_op jit(solution)/shard_map/all_gather | solution.py:61
  106.2 187.5 %all-reduce.7.cloned.1.call-start = ((), (), s32[]{:S(2)}) async-start(), calls=%async_computation.1 | async-start | bytes 163840 | tf_op jit(solution)/shard_map/psum | solution.py:87
  106.2 2.5 copy-start.5
  108.7 57.3 %copy-start = (bf16[2,160,1280]{2,1,0:T(8,128)(2,1)S(1)}, bf16[2,160,1280]{2,1,0:T(8,128)(2,1)}, u32[]{:S(2)}) copy-start(bf16[2,160,1280]{2,1,0:T(8,128)(2,1)} %param.23) | copy-start | bytes 2457604
  168.3 125.4 %copy-start.1 = (f32[16,1280]{1,0:T(8,128)S(1)}, f32[16,1280]{1,0:T(8,128)}, u32[]{:S(2)}) copy-start(f32[16,1280]{1,0:T(8,128)} %all-reduce.5.cloned.1.call-done) | copy-start | bytes 245764
  168.3 195.9 %all-reduce.9.cloned.1.call-start = ((), (), s32[]{:S(2)}) async-start(), calls=%async_computation.2 | async-start | bytes 163840 | tf_op jit(solution)/shard_map/psum | solution.py:87
  308.0 115.5 %all-reduce.11.cloned.1.call-start = ((), (), s32[]{:S(2)}) async-start(), calls=%async_computation.3 | async-start | bytes 163840 | tf_op jit(solution)/shard_map/psum | solution.py:87
Sparse Core Ops, SparseCore 0:
  10.2 71.6 all-gather.4
  105.6 59.4 all-reduce.4
  167.2 68.3 all-gather.6
  237.7 55.9 all-reduce.6
  308.1 55.9 all-reduce.8
  367.5 55.9 all-reduce.10
where the time goes:
time: 433 us; the launch traced here: 432 us
  waiting for transfers between devices  286 us (66%)
  local copies, waits for them, and re-layouts  103 us (24%)
  matrix products  21.1 us (5%)
  between operations  14.4 us (3%)
  other arithmetic  7.59 us (2%)
    psum x4, waiting for transfers between devices, add_branch(): residual = residual + lax.psum(partial_value, 'head')  218 us
    gather x1, local copies, waits for them, and re-layouts, page_groups(): return jnp.repeat(owners, page_len, total_repeat_length=count * page_len)  73 us
    all_gather x2, waiting for transfers between devices, attend(): piece = lax.all_gather(layer_prompt, 'req', axis=1, tiled=True)  67.2 us
    slice x2, local copies, waits for them, and re-layouts, attend(): keys = piece[0].reshape(count, head_count, HD, page_len)  9.05 us
  transfers between devices with their start and end apart: 6, of which 5 were waited for; matrix products, arithmetic and copies ran while one was open for 24% of the time, Pallas kernels for 0%

commit v1 on v0

--- a/solution.py
+++ b/solution.py
@@ -7,6 +7,15 @@
 HD = 80
 PPAGES = 4
 NEG_FLOOR = -1e30
+
+
+def feed_roots_for(dim_at, here_x):
+    grid = []
+    for _ in range(lax.axis_size("req")):
+        grid.append(here_x)
+    return jnp.concatenate(
+        lax.all_to_all(jnp.stack(grid), "req", split_axis=0, concat_axis=0), axis=dim_at
+    )
 
 
 def root_norm(values, gains):
@@ -58,7 +67,7 @@
         val_heads,
         preferred_element_type=jnp.float32,
     )
-    piece = lax.all_gather(layer_prompt, "req", axis=1, tiled=True)
+    piece = feed_roots_for(1, layer_prompt)
     count = piece.shape[1]
     key_group = page_groups(prompt_owner, count, page_len)
     keys = piece[0].reshape(count, head_count, HD, page_len)

time: 433 us -> 474 us (1.095)
  blocking collectives: 0 us -> 97.4 us
  waiting for transfers between devices: 286 us -> 213 us
  local copies, waits for them, and re-layouts: 103 us -> 115 us
  starting transfers between devices: 0.24 us -> 5.18 us
    all_to_all x0 -> x1, blocking collectives: none -> 97.4 us  [feed_roots_for(): lax.all_to_all(jnp.stack(grid), 'req', split_axis=0, concat_axis=0)]
    all_gather x2 -> x0, waiting for transfers between devices: 67.2 us -> none  [attend(): piece = lax.all_gather(layer_prompt, 'req', axis=1, tiled=True)]
    psum x4, waiting for transfers between devices: 218 us -> 199 us  [add_branch(): residual = residual + lax.psum(partial_value, 'head')]
    all_to_all x0 -> x1, waiting for transfers between devices: none -> 14.6 us  [feed_roots_for(): lax.all_to_all(jnp.stack(grid), 'req', split_axis=0, concat_axis=0)]
    all_to_all x0 -> x2, local copies, waits for them, and re-layouts: none -> 12.4 us  [feed_roots_for(): lax.all_to_all(jnp.stack(grid), 'req', split_axis=0, concat_axis=0)]
    another operation x0 -> x2, local copies, waits for them, and re-layouts: none -> 6.69 us  [feed_roots_for(): jnp.stack(grid)]
    all_to_all x0 -> x1, starting transfers between devices: none -> 4.83 us  [feed_roots_for(): lax.all_to_all(jnp.stack(grid), 'req', split_axis=0, concat_axis=0)]
  transfers between devices with their start and end apart: 6 -> 5, of which waited for: 5 -> 5; matrix products, arithmetic and copies ran while one was open for 24% -> 24% of each run, Pallas kernels for 0% -> 0%
where the time goes in v1:
time: 474 us; the launch traced here: 473 us
  waiting for transfers between devices  213 us (45%)
  local copies, waits for them, and re-layouts  115 us (24%)
  blocking collectives  97.4 us (21%)
  matrix products  20.1 us (4%)
  between operations  14.1 us (3%)
  other arithmetic  7.6 us (2%)
  starting transfers between devices  5.18 us (1%)
    psum x4, waiting for transfers between devices, add_branch(): residual = residual + lax.psum(partial_value, 'head')  199 us
    all_to_all x1, blocking collectives, feed_roots_for(): lax.all_to_all(jnp.stack(grid), 'req', split_axis=0, concat_axis=0)  97.4 us
    gather x1, local copies, waits for them, and re-layouts, page_groups(): return jnp.repeat(owners, page_len, total_repeat_length=count * page_len)  73 us
    all_to_all x1, waiting for transfers between devices, feed_roots_for(): lax.all_to_all(jnp.stack(grid), 'req', split_axis=0, concat_axis=0)  14.6 us
    all_to_all x2, local copies, waits for them, and re-layouts, feed_roots_for(): lax.all_to_all(jnp.stack(grid), 'req', split_axis=0, concat_axis=0)  12.4 us
  transfers between devices with their start and end apart: 5, of which 5 were waited for; matrix products, arithmetic and copies ran while one was open for 24% of the time, Pallas kernels for 0%

profile of v1, /device:TPU:1, one launch (start us, length us, event | category | flops | bytes accessed | tf_op | source)
XLA Modules:
  0.0 473.1 jit_solution(3040093771078235490)
XLA Ops:
  7.2 1.2 slice_bitcast_fusion.2
  8.4 1.8 stack.21
  10.2 97.4 %all_to_all.10 = bf16[16,2,6,160,128]{4,3,2,1,0:T(8,128)(2,1)} all-to-all(bf16[16,2,6,160,128]{4,3,2,1,0:T(8,128)(2,1)S(1)} %stack.21), channel_id=1, replica_groups=mesh['req'=16,'head'=8] {'req'}, dimensions={0} | all-to-all | bytes 15728640 | tf_op jit(solution)/shard_map/all_to_all | solution.py:17
  107.6 4.9 %stack.22 = bf16[16,2,6,160,128]{4,3,2,1,0:T(8,128)(2,1)} broadcast(bf16[2,6,160,128]{3,2,1,0:T(8,128)(2,1)S(1)} %get-tuple-element.57), dimensions={1,2,3,4} | broadcast | bytes 8355840 | tf_op jit(solution)/shard_map/stack | solution.py:17
  112.5 4.8 %all-to-all-start.1 = ((bf16[16,2,6,160,128]{4,3,2,1,0:T(8,128)(2,1)}), bf16[16,2,6,160,128]{4,3,2,1,0:T(8,128)(2,1)}, u32[]{:S(2)}, u32[]{:S(2)}) async-start(bf16[16,2,6,160,128]{4,3,2,1,0:T(8,128)(2,1)} %stack.22), calls=%async_computation.1 | async-start | bytes 15728640 | tf_op jit(solution)/shard_map/all_to_all | solution.py:17
  117.6 0.5 fusion.38
  118.5 0.5 broadcast.284
  119.1 0.7 reduce.26
  120.0 4.5 slice_bitcast_fusion
  124.5 4.2 gather_fusion
  128.7 2.4 gather_fusion.1
  131.1 73.0 %gather_fusion.2 = s32[12288]{0:T(1024)S(1)} fusion(s32[96]{0:T(128)S(1)} %and_select_fusion, s32[12288]{0:T(1024)S(1)} %fusion.97), kind=kCustom, calls=%fused_computation.clone | custom fusion | bytes 147456 | tf_op jit(solution)/shard_map/jit(_take)/gather | solution.py:28
  204.2 0.3 fusion.146
  204.6 0.3 fusion.26
  205.0 0.2 fusion.116
  205.2 0.2 broadcast_compare_fusion
  205.4 0.4 fusion.24
  205.8 0.6 copy-done
  206.3 1.3 fusion.145
  207.6 4.6 copy.180
  212.2 0.6 fusion.144
  212.8 0.8 fusion.11
  213.6 0.5 fusion.28
  214.2 1.2 fusion.62
  215.5 0.8 fusion.86
  216.4 14.6 %all-to-all-done.1 = bf16[16,2,6,160,128]{4,3,2,1,0:T(8,128)(2,1)} async-done(((bf16[16,2,6,160,128]{4,3,2,1,0:T(8,128)(2,1)}), bf16[16,2,6,160,128]{4,3,2,1,0:T(8,128)(2,1)}, u32[]{:S(2)}, u32[]{:S(2)}) %all-to-all-start.1) | async-done | bytes 7864352 | tf_op jit(solution)/shard_map/all_to_all | solution.py:17
  231.0 7.8 %copy.179 = bf16[16,2,6,160,128]{4,3,2,0,1:T(8,128)(2,1)} copy(bf16[16,2,6,160,128]{4,3,2,1,0:T(8,128)(2,1)} %all-to-all-done.1) | data formatting | bytes 15728640 | tf_op jit(solution)/shard_map/all_to_all | solution.py:17
  238.8 36.8 %all-reduce.5.cloned.1.call-done = f32[16,1280]{1,0:T(8,128)} async-done(((f32[16,1280]{1,0:T(8,128)}), f32[16,1280]{1,0:T(8,128)}) %all-reduce.5.cloned.1.call-update) | async-done | bytes 81936 | tf_op jit(solution)/shard_map/psum | solution.py:96
  275.7 1.0 multiply_reduce_fusion.2
  276.7 2.2 fusion.82
  278.9 0.2 all-reduce.9.cloned.1.call-start
  279.2 5.5 %fusion.143 = (bf16[1,16,6,160,128]{4,3,2,1,0:T(8,128)(2,1)}, bf16[1,16,6,160,128]{4,3,2,1,0:T(8,128)(2,1)}) fusion(bf16[2,16,6,160,128]{4,3,2,1,0:T(8,128)(2,1)} %bitcast.212), kind=kLoop, calls=%fused_computation.181 | loop fusion | bytes 15728640 | tf_op jit(solution)/shard_map/slice | solution.py:73
  284.7 50.4 %all-reduce.7.cloned.1.call-done = f32[16,1280]{1,0:T(8,128)} async-done(((f32[16,1280]{1,0:T(8,128)}), f32[16,1280]{1,0:T(8,128)}) %all-reduce.7.cloned.1.call-update) | async-done | bytes 81936 | tf_op jit(solution)/shard_map/psum | solution.py:96
  335.1 1.0 multiply_reduce_fusion.1
  336.1 1.7 fusion.41
  338.4 0.3 fusion.22
  338.7 0.2 fusion.118
  338.9 2.9 fusion.8
  341.9 1.8 fusion.20
  343.6 0.6 fusion.30
  344.2 3.4 fusion.65
  347.7 1.8 fusion.80
  349.6 56.1 %all-reduce.9.cloned.1.call-done = f32[16,1280]{1,0:T(8,128)} async-done(((f32[16,1280]{1,0:T(8,128)}), f32[16,1280]{1,0:T(8,128)}) %all-reduce.9.cloned.1.call-update) | async-done | bytes 81936 | tf_op jit(solution)/shard_map/psum | solution.py:96
  405.7 1.0 multiply_reduce_fusion
  406.7 2.2 fusion.76
  408.9 0.6 copy.62
  409.5 55.5 %all-reduce.11.cloned.1.call-done = f32[16,1280]{1,0:T(8,128)} async-done(((f32[16,1280]{1,0:T(8,128)}), f32[16,1280]{1,0:T(8,128)}) %all-reduce.11.cloned.1.call-update) | async-done | bytes 81936 | tf_op jit(solution)/shard_map/psum | solution.py:96
  465.0 1.5 add_convert_fusion
  (78 shorter events, 2.4 us)
Async XLA Ops:
  112.5 4.9 %copy-start.8 = (f32[2,1280]{1,0:T(2,128)S(1)}, f32[2,1280]{1,0:T(2,128)}, u32[]{:S(2)}) copy-start(f32[2,1280]{1,0:T(2,128)} %param.24) | copy-start | bytes 30724
  112.5 5.0 %copy-start.6 = (bf16[16,1280]{1,0:T(8,128)(2,1)S(1)}, bf16[16,1280]{1,0:T(8,128)(2,1)}, u32[]{:S(2)}) copy-start(bf16[16,1280]{1,0:T(8,128)(2,1)} %param.19) | copy-start | bytes 122884
  112.5 5.1 %copy-start.7 = (bf16[2,3,160,1280]{3,2,1,0:T(8,128)(2,1)S(1)}, bf16[2,3,160,1280]{3,2,1,0:T(8,128)(2,1)}, u32[]{:S(2)}) copy-start(bf16[2,3,160,1280]{3,2,1,0:T(8,128)(2,1)} %param.20) | copy-start | bytes 7372804
  112.5 118.5 %all-to-all-start.1 = ((bf16[16,2,6,160,128]{4,3,2,1,0:T(8,128)(2,1)}), bf16[16,2,6,160,128]{4,3,2,1,0:T(8,128)(2,1)}, u32[]{:S(2)}, u32[]{:S(2)}) async-start(bf16[16,2,6,160,128]{4,3,2,1,0:T(8,128)(2,1)} %stack.22), calls=%async_computation.1 | async-start | bytes 15728640 | tf_op jit(solution)/shard_map/all_to_all | solution.py:17
  117.3 1.7 copy-start.12
  117.4 158.3 %all-reduce.5.cloned.1.call-start = ((), (), s32[]{:S(2)}) async-start(), calls=%async_computation.2 | async-start | bytes 163840 | tf_op jit(solution)/shard_map/psum | solution.py:96
  128.7 2.4 copy-start.13
  131.1 73.1 %copy-start.11 = (s32[16]{0:T(128)S(1)}, s32[16]{0:T(128)}, u32[]{:S(2)}) copy-start(s32[16]{0:T(128)} %param.30) | copy-start | bytes 196
  131.1 73.2 %copy-start.1 = (bf16[32,2,160,128]{3,2,1,0:T(8,128)(2,1)S(1)}, bf16[32,2,160,128]{3,2,1,0:T(8,128)(2,1)}, u32[]{:S(2)}) copy-start(bf16[32,2,160,128]{3,2,1,0:T(8,128)(2,1)} %gather_fusion) | copy-start | bytes 7864324
  204.2 0.9 copy-start.10
  204.6 1.7 copy-start
  214.1 1.4 copy-start.4
  214.1 2.2 copy-start.9
  216.3 118.8 %all-reduce.7.cloned.1.call-start = ((), (), s32[]{:S(2)}) async-start(), calls=%async_computation.3 | async-start | bytes 163840 | tf_op jit(solution)/shard_map/psum | solution.py:96
  216.4 60.3 %copy-start.2 = (bf16[2,160,1280]{2,1,0:T(8,128)(2,1)S(1)}, bf16[2,160,1280]{2,1,0:T(8,128)(2,1)}, u32[]{:S(2)}) copy-start(bf16[2,160,1280]{2,1,0:T(8,128)(2,1)} %param.23) | copy-start | bytes 2457604
  278.9 126.7 %all-reduce.9.cloned.1.call-start = ((), (), s32[]{:S(2)}) async-start(), calls=%async_computation.4 | async-start | bytes 163840 | tf_op jit(solution)/shard_map/psum | solution.py:96
  279.2 55.9 %copy-start.5 = (f32[16,1280]{1,0:T(8,128)S(1)}, f32[16,1280]{1,0:T(8,128)}, u32[]{:S(2)}) copy-start(f32[16,1280]{1,0:T(8,128)} %all-reduce.5.cloned.1.call-done) | copy-start | bytes 245764
  344.2 62.5 %copy-start.3 = (bf16[2,160,1280]{2,1,0:T(8,128)(2,1)S(1)}, bf16[2,160,1280]{2,1,0:T(8,128)(2,1)}, u32[]{:S(2)}) copy-start(bf16[2,160,1280]{2,1,0:T(8,128)(2,1)} %param.23) | copy-start | bytes 2457604
  349.5 115.5 %all-reduce.11.cloned.1.call-start = ((), (), s32[]{:S(2)}) async-start(), calls=%async_computation.5 | async-start | bytes 163840 | tf_op jit(solution)/shard_map/psum | solution.py:96
Sparse Core Ops, SparseCore 0:
  216.4 59.1 all-reduce.4
  279.1 55.9 all-reduce.6
  349.6 55.9 all-reduce.8
  409.0 55.9 all-reduce.10
